TPU v7x, 32 devices: a whole 2x2x4 slice. The times are simulated.
32 devices in a mesh: dp: 2 (over y), expert: 16 (over z, x, core).
Axes of the slice: x: 2, y: 2, z: 4, core: 2. Of those that a mesh axis runs over, the one named last changes fastest.
Arguments:
- attention: bfloat16 [16, 2, 16, 1024], P('expert', 'dp'), may hold values from -6 to 6
- residual: bfloat16 [16, 2, 16, 2048], P('expert', 'dp')
- out_proj: bfloat16 [1024, 2048], P(None, 'dp'), may hold values from -0.1875 to 0.1875
- gain_in: float32 [2048], replicated, may hold values from 0.5 to 1.5
- router: bfloat16 [2048, 16], P(None, 'dp')
- expert_ids: int32 [16, 2, 16, 6], P('expert'), may hold values from 0 to 15, all different within a row; in each aligned block of 16 rows (0 to 15, 16 to 31, ..., all dimensions but the last counted through in order) at most 12 rows name the same one
- live_rows: int32 [2, 16], P(None, 'expert'), may hold values from 1 to 16, 224 in all within a row
- expert_gate: bfloat16 [16, 1408, 2048], P('expert', 'dp'), may hold values from -0.25 to 0.25
- expert_up: bfloat16 [16, 1408, 2048], P('expert', 'dp'), may hold values from -0.25 to 0.25
- expert_down: bfloat16 [16, 1408, 2048], P('expert', None, 'dp'), may hold values from -0.15625 to 0.15625
- shared_gate: bfloat16 [1408, 2048], P('dp'), may hold values from -0.125 to 0.125
- shared_up: bfloat16 [1408, 2048], P('dp'), may hold values from -0.125 to 0.125
- shared_down: bfloat16 [1408, 2048], P(None, 'dp'), may hold values from -0.15625 to 0.15625
- gain_out: float32 [2048], replicated, may hold values from 0.5 to 1.5
Outputs:
- stream: bfloat16 [16, 2, 16, 2048], P('expert', 'dp')
- normed: bfloat16 [16, 2, 16, 2048], P('expert', 'dp')
Inputs may be any that keep to these rules, and one draw needn't show every extreme that they name: `expert_ids`: each row names 6 different experts; the 16 rows of one block [o, g] name one expert at most 12 times, a bound that some block reaches. The live rows of a device are its first live_rows[g, o]; the 16 counts of each g sum to 224, and one of them is 16.
All inputs are finite; a program needn't handle non-finite values.
Results may differ from a plain program's by a relative error of at most 0.0095.
Values may be sent and summed in bfloat16 or wider, within the bound.
No kernel may reach another device: no remote copies, remote signals or barrier semaphores. Data moves between devices by JAX's collectives and lax.ppermute only.
A program may use at most 128 MiB of HBM per device.

v0:
```python
import jax
import jax.numpy as jnp
from jax import lax
from jax.sharding import PartitionSpec as P


def rms_scale(features, scale_gain):
    return (
        features
        * lax.rsqrt(jnp.mean(features * features, axis=-1, keepdims=True) + 1e-06)
        * scale_gain
    )


def by_rows(left, weight_rows):
    return lax.dot_general(
        left, weight_rows, (((1,), (1,)), ((), ())), preferred_element_type=jnp.float32
    )


def gather_axis(x, name, axis):
    n = lax.axis_size(name)
    if n == 1:
        return x
    me = lax.axis_index(name)
    pieces = [x]
    for shift in range(1, n):
        pieces.append(lax.ppermute(x, name, [(j, (j + shift) % n) for j in range(n)]))
    if n == 2:
        first = jnp.where(me == 0, pieces[0], pieces[1])
        second = jnp.where(me == 0, pieces[1], pieces[0])
        ordered = [first, second]
        return jnp.concatenate(ordered, axis=axis)
    stacked = jnp.stack(pieces, 0)
    order = (me - jnp.arange(n)) % n
    ordered = jnp.take(stacked, order, axis=0)
    ordered = jnp.moveaxis(ordered, 0, axis)
    shape = list(x.shape)
    shape[axis] = shape[axis] * n
    return ordered.reshape(shape)


def shards(
    attention,
    residual,
    out_proj,
    gain_in,
    router,
    expert_ids,
    live_rows,
    expert_gate,
    expert_up,
    expert_down,
    shared_gate,
    shared_up,
    shared_down,
    gain_out,
):
    groups = lax.axis_size("dp")
    experts = lax.axis_size("expert")
    row_count = attention.shape[2]
    feature_width = residual.shape[3]
    top_count = expert_ids.shape[3]
    capacity = max(2, (2 * row_count * top_count + experts - 1) // experts)
    gate_local = expert_gate[0]
    up_local = expert_up[0]
    down_local = expert_down[0]
    column_width = down_local.shape[1]
    rows_all = groups * row_count
    pieces = gather_axis(attention, "dp", 1)
    flattened = pieces.reshape(-1, pieces.shape[-1])
    product = jnp.dot(flattened, out_proj, preferred_element_type=jnp.float32).astype(jnp.bfloat16)
    columns = product.reshape(pieces.shape[:-1] + (out_proj.shape[1],))
    projected = lax.all_to_all(columns, "dp", split_axis=1, concat_axis=3, tiled=True)[0, 0]
    stream_in = residual[0, 0].astype(jnp.float32) + projected.astype(jnp.float32)
    normal_rows = rms_scale(stream_in, gain_in).astype(jnp.bfloat16)
    column = gather_axis(normal_rows, "dp", 0)
    logit_part = jnp.dot(column, router, preferred_element_type=jnp.float32)
    logits = gather_axis(logit_part, "dp", 1)
    flat_experts = expert_ids[0].reshape(rows_all, top_count)
    picked = jnp.take_along_axis(logits, flat_experts, axis=1)
    probabilities = jax.nn.softmax(picked, axis=1)
    row_live = (jnp.arange(row_count, dtype=jnp.int32)[None, :] < live_rows[:, 0][:, None]).reshape(
        rows_all
    )
    slot_live = jnp.broadcast_to(row_live[:, None], (rows_all, top_count))
    weights = probabilities.astype(jnp.bfloat16) * slot_live.astype(jnp.bfloat16)
    block_experts = flat_experts.reshape(groups, row_count * top_count)
    block_live = slot_live.reshape(groups, row_count * top_count)
    onehot = (
        (block_experts[:, :, None] == jnp.arange(experts, dtype=jnp.int32)) & block_live[:, :, None]
    ).astype(jnp.int32)
    before = jnp.cumsum(onehot, axis=1) - onehot
    position = jnp.sum(before * onehot, axis=2)
    slot_total = experts * groups * capacity
    offsets = jnp.arange(groups, dtype=jnp.int32)[:, None] * capacity
    target = jnp.where(
        block_live, block_experts * (groups * capacity) + offsets + position, slot_total
    ).reshape(rows_all, top_count)
    slot_hit = target[:, :, None] == jnp.arange(slot_total, dtype=jnp.int32)[None, None, :]
    fill = jnp.any(slot_hit, axis=1).astype(jnp.bfloat16)
    outgoing = (
        lax.dot_general(fill, column, (((0,), (0,)), ((), ())), preferred_element_type=jnp.float32)
        .astype(jnp.bfloat16)
        .reshape(experts, groups * capacity, feature_width)
    )
    slot_rows = lax.all_to_all(outgoing, "expert", split_axis=0, concat_axis=0, tiled=True)
    flattened = slot_rows.reshape(-1, slot_rows.shape[-1])
    gate_value = by_rows(flattened, gate_local)
    up_value = by_rows(flattened, up_local)
    hidden = (jax.nn.silu(gate_value) * up_value).astype(jnp.bfloat16)
    shared_gate_value = by_rows(column, shared_gate)
    shared_up_value = by_rows(column, shared_up)
    shared_hidden = (jax.nn.silu(shared_gate_value) * shared_up_value).astype(jnp.bfloat16)
    routed_piece = gather_axis(hidden, "dp", 1)
    shared_piece = gather_axis(shared_hidden, "dp", 1)
    routed_total = jnp.dot(routed_piece, down_local, preferred_element_type=jnp.float32)
    shared = jnp.dot(shared_piece, shared_down, preferred_element_type=jnp.float32)
    expert_out = routed_total.astype(jnp.bfloat16).reshape(experts, groups * capacity, column_width)
    returned = lax.all_to_all(
        expert_out, "expert", split_axis=0, concat_axis=0, tiled=True
    ).reshape(slot_total, column_width)
    combine = jnp.sum(
        jnp.where(slot_hit, weights[:, :, None], jnp.zeros((), jnp.bfloat16)), axis=1
    ).astype(jnp.bfloat16)
    routed = jnp.dot(combine, returned, preferred_element_type=jnp.float32)
    combined = jnp.where(row_live[:, None], routed + shared, 0.0).reshape(
        groups, row_count, column_width
    )
    summed = lax.all_to_all(combined, "dp", split_axis=0, concat_axis=2, tiled=True)[0]
    stream_sum = stream_in + summed
    stream = stream_sum.astype(jnp.bfloat16)[None, None]
    normed = rms_scale(stream_sum, gain_out).astype(jnp.bfloat16)[None, None]
    return (stream, normed)


def solution(mesh):
    placed = (
        P("expert", "dp", None, None),
        P("expert", "dp", None, None),
        P(None, "dp"),
        P(),
        P(None, "dp"),
        P("expert", None, None, None),
        P(None, "expert"),
        P("expert", "dp", None),
        P("expert", "dp", None),
        P("expert", None, "dp"),
        P("dp", None),
        P("dp", None),
        P(None, "dp"),
        P(),
    )
    return jax.shard_map(
        shards,
        mesh=mesh,
        in_specs=placed,
        out_specs=(P("expert", "dp", None, None), P("expert", "dp", None, None)),
        check_vma=False,
    )
```

profile of v0, /device:TPU:0, one launch (start us, length us, event | category | flops | bytes accessed | tf_op | source)
XLA Modules:
  0.0 128.7 jit_solution(17526194311899023386)
XLA Ops:
  0.7 3.0 %collective-permute-start = (bf16[1,1,16,1024]{3,2,1,0:T(8,128)(2,1)}, bf16[1,1,16,1024]{3,2,1,0:T(8,128)(2,1)S(1)}, u32[]{:S(2)}, u32[]{:S(2)}) collective-permute-start(bf16[1,1,16,1024]{3,2,1,0:T(8,128)(2,1)} %param.14), channel_id=1, source_target_pairs={{0,16},{16,0},{1,17},{17,1},{2,18},{18,2},{3,19},{19,3},{4,20},{20... | collective-permute-start | bytes 98312 | tf_op jit(solution)/shard_map/ppermute | solution.py:28
  7.9 2.7 %convolution_convert_fusion.1 = bf16[32,1024]{1,0:T(8,128)(2,1)} fusion(bf16[32,1024]{1,0:T(8,128)(2,1)S(1)} %bitcast.92, bf16[1024,1024]{1,0:T(8,128)(2,1)} %param.16), kind=kOutput, calls=%fused_computation.13 | convolution fusion | flops 67141632 | bytes 2228224 | tf_op jit(solution)/shard_map/dot_general | solution.py:72
  10.6 3.3 %all-to-all-start = ((bf16[1,2,16,1024]{3,2,0,1:T(8,128)(2,1)}), bf16[1,2,16,1024]{3,2,0,1:T(8,128)(2,1)S(1)}, u32[]{:S(2)}, u32[]{:S(2)}) async-start(bf16[1,2,16,1024]{3,2,0,1:T(8,128)(2,1)} %bitcast.2), calls=%async_computation | async-start | bytes 131072 | tf_op jit(solution)/shard_map/all_to_all | solution.py:74
  14.0 4.1 %all-to-all-done = bf16[1,2,16,1024]{3,2,0,1:T(8,128)(2,1)S(1)} async-done(((bf16[1,2,16,1024]{3,2,0,1:T(8,128)(2,1)}), bf16[1,2,16,1024]{3,2,0,1:T(8,128)(2,1)S(1)}, u32[]{:S(2)}, u32[]{:S(2)}) %all-to-all-start) | async-done | bytes 65568 | tf_op jit(solution)/shard_map/all_to_all | solution.py:74
  18.6 4.1 %collective-permute-done.1 = bf16[16,2048]{1,0:T(8,128)(2,1)S(1)} collective-permute-done((bf16[16,2048]{1,0:T(8,128)(2,1)S(1)}, bf16[16,2048]{1,0:T(8,128)(2,1)S(1)}, u32[]{:S(2)}, u32[]{:S(2)}) %collective-permute-start.1) | collective-permute-done | bytes 65568 | tf_op jit(solution)/shard_map/ppermute | solution.py:28
  23.4 41.9 %all_to_all.34 = bf16[16,24,2048]{2,1,0:T(8,128)(2,1)S(1)} all-to-all(bf16[16,24,2048]{2,1,0:T(8,128)(2,1)S(1)} %bitcast.83), channel_id=1, replica_groups=mesh['dp'=2,'expert'=16] {'expert'}, dimensions={0} | all-to-all | bytes 3145728 | tf_op jit(solution)/shard_map/all_to_all | solution.py:107
  65.3 1.7 %fusion.4 = f32[384,704]{0,1:T(8,128)S(1)} fusion(bf16[384,2048]{1,0:T(8,128)(2,1)S(1)} %bitcast.84, bf16[1,704,2048]{2,1,0:T(8,128)(2,1)S(1)} %copy-done.4), kind=kOutput, calls=%fused_computation.5 | convolution fusion | flops 1107296256 | bytes 5537792 | tf_op jit(solution)/shard_map/dot_general | solution.py:16
  67.2 2.5 %fusion.12 = bf16[384,704]{0,1:T(8,128)(2,1)} fusion(bf16[384,2048]{1,0:T(8,128)(2,1)S(1)} %bitcast.85, bf16[1,704,2048]{2,1,0:T(8,128)(2,1)S(1)} %copy-done.5, f32[384,704]{0,1:T(8,128)S(1)} %fusion.4), kind=kOutput, calls=%fused_computation.10 | convolution fusion | flops 1108918272 | bytes 6078464 | tf_op jit(solution)/shard_map/dot_general | solution.py:16
  70.0 2.7 %fusion.39 = f32[32,704]{1,0:T(8,128)S(1)} fusion(bf16[704,2048]{1,0:T(8,128)(2,1)} %param.24, bf16[16,2048]{1,0:T(8,128)(2,1)S(1)} %get-tuple-element.9, bf16[16,2048]{1,0:T(8,128)(2,1)S(1)} %get-tuple-element.8), kind=kOutput, calls=%fused_computation.73 | convolution fusion | flops 92536832 | bytes 3104768 | tf_op jit(solution)/shard_map/dot_general | solution.py:16
  72.7 12.2 %collective-permute-done.3 = bf16[384,704]{0,1:T(8,128)(2,1)} collective-permute-done((bf16[384,704]{0,1:T(8,128)(2,1)}, bf16[384,704]{0,1:T(8,128)(2,1)}, u32[]{:S(2)}, u32[]{:S(2)}) %collective-permute-start.3) | collective-permute-done | bytes 540704 | tf_op jit(solution)/shard_map/ppermute | solution.py:28
  84.9 1.3 %broadcast_select_fusion.1 = (bf16[384,704]{0,1:T(8,128)(2,1)S(1)}, bf16[384,704]{0,1:T(8,128)(2,1)S(1)}) fusion(bf16[384,704]{0,1:T(8,128)(2,1)} %fusion.12, bf16[384,704]{0,1:T(8,128)(2,1)} %collective-permute-done.3, pred[]{:T(512)S(6)} %eq.16), kind=kLoop, calls=%fused_computation.18 | loop fusion | flops 540672 | bytes 2162689 | tf_op jit(solution)/shard_map/jit(_where)/select_n | solution.py:30
  86.3 2.3 %fusion.6 = bf16[384,1024]{1,0:T(8,128)(2,1)} fusion(bf16[1,1408,1024]{2,1,0:T(8,128)(2,1)S(1)} %copy-done, bf16[384,704]{0,1:T(8,128)(2,1)S(1)} %get-tuple-element.3, bf16[384,704]{0,1:T(8,128)(2,1)S(1)} %get-tuple-element.2), kind=kOutput, calls=%fused_computation.8 | convolution fusion | flops 1109852160 | bytes 4751360 | tf_op jit(solution)/shard_map/dot_general | solution.py:117
  88.6 4.6 %all-to-all-start.2 = ((bf16[16,24,1024]{2,1,0:T(8,128)(2,1)}), bf16[16,24,1024]{2,1,0:T(8,128)(2,1)}, u32[]{:S(2)}, u32[]{:S(2)}) async-start(bf16[16,24,1024]{2,1,0:T(8,128)(2,1)} %bitcast.90), calls=%async_computation.2 | async-start | bytes 1572864 | tf_op jit(solution)/shard_map/all_to_all | solution.py:120
  93.7 2.7 %multiply_convert_fusion.2 = bf16[32,704]{1,0:T(8,128)(2,1)S(1)} fusion(f32[32,704]{1,0:T(8,128)S(1)} %fusion.39, bf16[704,2048]{1,0:T(8,128)(2,1)} %param.25, bf16[16,2048]{1,0:T(8,128)(2,1)S(1)} %get-tuple-element.9, bf16[16,2048]{1,0:T(8,128)(2,1)S(1)} %get-tuple-element.8), kind=kOutput, calls=%fused_computation.35 | convolution fusion | flops 92672000 | bytes 3149824 | tf_op jit(solution)/shard_map/dot_general | solution.py:16
  96.4 1.8 %collective-permute-start.4 = (bf16[32,704]{1,0:T(8,128)(2,1)S(1)}, bf16[32,704]{1,0:T(8,128)(2,1)S(1)}, u32[]{:S(2)}, u32[]{:S(2)}) collective-permute-start(bf16[32,704]{1,0:T(8,128)(2,1)S(1)} %multiply_convert_fusion.2), channel_id=1, source_target_pairs={{0,16},{16,0},{1,17},{17,1},{2,18},{18,2},{3,19},{19,3},{4,20},{20... | collective-permute-start | bytes 135176 | tf_op jit(solution)/shard_map/ppermute | solution.py:28
  98.2 1.7 %gather_fusion = f32[192]{0:T(256)S(1)} fusion(f32[32,16]{0,1:T(8,128)S(1)} %pad_maximum_fusion.2, s32[192]{0:T(256)S(1)} %reshape.303), kind=kCustom, calls=%fused_computation | custom fusion | bytes 3072 | tf_op jit(solution)/shard_map/jit(take_along_axis)/gather | solution.py:81
  100.8 11.2 %all-to-all-done.2 = bf16[16,24,1024]{2,1,0:T(8,128)(2,1)} async-done(((bf16[16,24,1024]{2,1,0:T(8,128)(2,1)}), bf16[16,24,1024]{2,1,0:T(8,128)(2,1)}, u32[]{:S(2)}, u32[]{:S(2)}) %all-to-all-start.2) | async-done | bytes 786464 | tf_op jit(solution)/shard_map/all_to_all | solution.py:120
  112.0 1.4 %fusion.42 = f32[32,1024]{1,0:T(8,128)S(1)} fusion(bf16[32,384]{1,0:T(8,128)(2,1)S(1)} %fusion.21, bf16[384,1024]{1,0:T(8,128)(2,1)} %bitcast.14), kind=kOutput, calls=%fused_computation.76 | convolution fusion | flops 25165824 | bytes 942080 | tf_op jit(solution)/shard_map/dot_general | solution.py:126
  113.3 3.1 %fusion.15 = f32[32,1024]{1,0:T(8,128)} fusion(f32[32,1024]{1,0:T(8,128)S(1)} %fusion.42, bf16[1408,1024]{1,0:T(8,128)(2,1)} %param.26, bf16[32,704]{1,0:T(8,128)(2,1)S(1)} %get-tuple-element.11, bf16[32,704]{1,0:T(8,128)(2,1)S(1)} %get-tuple-element.10, pred[32]{0:T(512)(128)(4,1)S(1)} %lt.57), kind=kOutput, calls=%fused_computation.12 | convolution fusion | flops 92520448 | bytes 3235872 | tf_op jit(solution)/shard_map/dot_general | solution.py:118
  116.4 3.4 %all-to-all-start.3 = ((f32[2,16,1024]{2,1,0:T(8,128)}), f32[2,16,1024]{2,1,0:T(8,128)S(1)}, u32[]{:S(2)}, u32[]{:S(2)}) async-start(f32[2,16,1024]{2,1,0:T(8,128)} %bitcast.15), calls=%async_computation.3 | async-start | bytes 262144 | tf_op jit(solution)/shard_map/all_to_all | solution.py:130
  120.7 3.5 %all-to-all-done.3 = f32[2,16,1024]{2,1,0:T(8,128)S(1)} async-done(((f32[2,16,1024]{2,1,0:T(8,128)}), f32[2,16,1024]{2,1,0:T(8,128)S(1)}, u32[]{:S(2)}, u32[]{:S(2)}) %all-to-all-start.3) | async-done | bytes 131104 | tf_op jit(solution)/shard_map/all_to_all | solution.py:130
  125.0 1.0 squeeze.17
  126.1 1.2 fusion.24
  127.2 1.4 %multiply_convert_fusion = (bf16[1,1,16,2048]{3,2,1,0:T(8,128)(2,1)}, bf16[1,1,16,2048]{3,2,1,0:T(8,128)(2,1)}) fusion(f32[2048]{0:T(1024)} %param.27, f32[16]{0:T(128)S(1)} %add_rsqrt_fusion, f32[1,1,16,2048]{3,2,1,0:T(8,128)S(1)} %squeeze.17, f32[1,1,16,2048]{3,2,1,0:T(8,128)S(1)} %reshape.295, bf16[1,1,16,2048]{3,2,1,0:T(8,128)(2,1)S(1)} %copy-done.1), kind=kLoop, calls=%fused_computation.30 | loop fusion | flops 229376 | bytes 467008 | tf_op jit(solution)/shard_map/convert_element_type | solution.py:133
  (69 shorter events, 8.8 us)
Async XLA Ops:
  0.6 85.6 %copy-start = (bf16[1,1408,1024]{2,1,0:T(8,128)(2,1)S(1)}, bf16[1,1408,1024]{2,1,0:T(8,128)(2,1)}, u32[]{:S(2)}) copy-start(bf16[1,1408,1024]{2,1,0:T(8,128)(2,1)} %param.23) | copy-start | bytes 8650756
  0.6 17.5 %copy-start.1 = (bf16[1,1,16,2048]{3,2,1,0:T(8,128)(2,1)S(1)}, bf16[1,1,16,2048]{3,2,1,0:T(8,128)(2,1)}, u32[]{:S(2)}) copy-start(bf16[1,1,16,2048]{3,2,1,0:T(8,128)(2,1)} %param.15) | copy-start | bytes 196612
  0.7 17.7 %copy-start.3 = (f32[2048]{0:T(1024)S(1)}, f32[2048]{0:T(1024)}, u32[]{:S(2)}) copy-start(f32[2048]{0:T(1024)} %param.17) | copy-start | bytes 24580
  0.7 6.5 %collective-permute-start = (bf16[1,1,16,1024]{3,2,1,0:T(8,128)(2,1)}, bf16[1,1,16,1024]{3,2,1,0:T(8,128)(2,1)S(1)}, u32[]{:S(2)}, u32[]{:S(2)}) collective-permute-start(bf16[1,1,16,1024]{3,2,1,0:T(8,128)(2,1)} %param.14), channel_id=1, source_target_pairs={{0,16},{16,0},{1,17},{17,1},{2,18},{18,2},{3,19},{19,3},{4,20},{20... | collective-permute-start | bytes 98312 | tf_op jit(solution)/shard_map/ppermute | solution.py:28
  10.6 7.4 %all-to-all-start = ((bf16[1,2,16,1024]{3,2,0,1:T(8,128)(2,1)}), bf16[1,2,16,1024]{3,2,0,1:T(8,128)(2,1)S(1)}, u32[]{:S(2)}, u32[]{:S(2)}) async-start(bf16[1,2,16,1024]{3,2,0,1:T(8,128)(2,1)} %bitcast.2), calls=%async_computation | async-start | bytes 131072 | tf_op jit(solution)/shard_map/all_to_all | solution.py:74
  18.4 4.3 %collective-permute-start.1 = (bf16[16,2048]{1,0:T(8,128)(2,1)S(1)}, bf16[16,2048]{1,0:T(8,128)(2,1)S(1)}, u32[]{:S(2)}, u32[]{:S(2)}) collective-permute-start(bf16[16,2048]{1,0:T(8,128)(2,1)S(1)} %multiply_convert_fusion.1), channel_id=1, source_target_pairs={{0,16},{16,0},{1,17},{17,1},{2,18},{18,2},{3,19},{19,3},{4,20},{20... | collective-permute-start | bytes 196616 | tf_op jit(solution)/shard_map/ppermute | solution.py:28
  22.8 42.6 %copy-start.4 = (bf16[1,704,2048]{2,1,0:T(8,128)(2,1)S(1)}, bf16[1,704,2048]{2,1,0:T(8,128)(2,1)}, u32[]{:S(2)}) copy-start(bf16[1,704,2048]{2,1,0:T(8,128)(2,1)} %param.21) | copy-start | bytes 8650756
  65.3 1.8 %copy-start.5 = (bf16[1,704,2048]{2,1,0:T(8,128)(2,1)S(1)}, bf16[1,704,2048]{2,1,0:T(8,128)(2,1)}, u32[]{:S(2)}) copy-start(bf16[1,704,2048]{2,1,0:T(8,128)(2,1)} %param.22) | copy-start | bytes 8650756
  67.2 2.5 %copy-start.2 = (s32[1,2,16,6]{2,1,3,0:T(2,128)S(1)}, s32[1,2,16,6]{2,1,3,0:T(2,128)}, u32[]{:S(2)}) copy-start(s32[1,2,16,6]{2,1,3,0:T(2,128)} %param.19) | copy-start | bytes 2308
  69.7 15.3 %collective-permute-start.3 = (bf16[384,704]{0,1:T(8,128)(2,1)}, bf16[384,704]{0,1:T(8,128)(2,1)}, u32[]{:S(2)}, u32[]{:S(2)}) collective-permute-start(bf16[384,704]{0,1:T(8,128)(2,1)} %fusion.12), channel_id=1, source_target_pairs={{0,16},{16,0},{1,17},{17,1},{2,18},{18,2},{3,19},{19,3},{4,20},{20... | collective-permute-start | bytes 1622024 | tf_op jit(solution)/shard_map/ppermute | solution.py:28
  86.2 7.0 %copy-start.6 = (bf16[2048,8]{0,1:T(8,128)(2,1)S(1)}, bf16[2048,8]{0,1:T(8,128)(2,1)}, u32[]{:S(2)}) copy-start(bf16[2048,8]{0,1:T(8,128)(2,1)} %param.18) | copy-start | bytes 98308
  88.6 23.4 %all-to-all-start.2 = ((bf16[16,24,1024]{2,1,0:T(8,128)(2,1)}), bf16[16,24,1024]{2,1,0:T(8,128)(2,1)}, u32[]{:S(2)}, u32[]{:S(2)}) async-start(bf16[16,24,1024]{2,1,0:T(8,128)(2,1)} %bitcast.90), calls=%async_computation.2 | async-start | bytes 1572864 | tf_op jit(solution)/shard_map/all_to_all | solution.py:120
  93.4 4.9 %collective-permute-start.2 = (f32[32,8]{0,1:T(8,128)S(1)}, f32[32,8]{0,1:T(8,128)S(1)}, u32[]{:S(2)}, u32[]{:S(2)}) collective-permute-start(f32[32,8]{0,1:T(8,128)S(1)} %fusion.40), channel_id=1, source_target_pairs={{0,16},{16,0},{1,17},{17,1},{2,18},{18,2},{3,19},{19,3},{4,20},{20... | collective-permute-start | bytes 3080 | tf_op jit(solution)/shard_map/ppermute | solution.py:28
  96.4 4.4 %collective-permute-start.4 = (bf16[32,704]{1,0:T(8,128)(2,1)S(1)}, bf16[32,704]{1,0:T(8,128)(2,1)S(1)}, u32[]{:S(2)}, u32[]{:S(2)}) collective-permute-start(bf16[32,704]{1,0:T(8,128)(2,1)S(1)} %multiply_convert_fusion.2), channel_id=1, source_target_pairs={{0,16},{16,0},{1,17},{17,1},{2,18},{18,2},{3,19},{19,3},{4,20},{20... | collective-permute-start | bytes 135176 | tf_op jit(solution)/shard_map/ppermute | solution.py:28
  116.4 7.8 %all-to-all-start.3 = ((f32[2,16,1024]{2,1,0:T(8,128)}), f32[2,16,1024]{2,1,0:T(8,128)S(1)}, u32[]{:S(2)}, u32[]{:S(2)}) async-start(f32[2,16,1024]{2,1,0:T(8,128)} %bitcast.15), calls=%async_computation.3 | async-start | bytes 262144 | tf_op jit(solution)/shard_map/all_to_all | solution.py:130
where the time goes:
time: 130 us; the launch traced here: 129 us
  blocking collectives  41.9 us (32%)
  waiting for transfers between devices  35.2 us (27%)
  matrix products  19.9 us (15%)
  starting transfers between devices  16.5 us (13%)
  other arithmetic  7.4 us (6%)
  local copies, waits for them, and re-layouts  6.88 us (5%)
    all_to_all x1, blocking collectives, shards(): lax.all_to_all(outgoing, 'expert', split_axis=0, concat_axis=0, tiled=True)  41.9 us
    ppermute x5, waiting for transfers between devices, gather_axis(): lax.ppermute(x, name, [(j, (j + shift) % n) for j in range(n)])  16.4 us
    all_to_all x1, waiting for transfers between devices, shards(): lax.all_to_all(expert_out, 'expert', split_axis=0, concat_axis=0, tiled=T...  11.2 us
    dot_general x4, matrix products, by_rows(): lax.dot_general(left, weight_rows, (((1,), (1,)), ((), ())), preferred_el...  9.61 us
    ppermute x5, starting transfers between devices, gather_axis(): lax.ppermute(x, name, [(j, (j + shift) % n) for j in range(n)])  5.24 us
    all_to_all x1, starting transfers between devices, shards(): lax.all_to_all(expert_out, 'expert', split_axis=0, concat_axis=0, tiled=T...  4.61 us
    all_to_all x1, waiting for transfers between devices, shards(): lax.all_to_all(columns, 'dp', split_axis=1, concat_axis=3, tiled=True)[0, 0]  4.09 us
    all_to_all x1, waiting for transfers between devices, shards(): lax.all_to_all(combined, 'dp', split_axis=0, concat_axis=2, tiled=True)[0]  3.53 us
  transfers between devices with their start and end apart: 8, of which 5 were waited for; matrix products, arithmetic and copies ran while one was open for 10% of the time, Pallas kernels for 0%

commit v1 on v0

--- a/solution.py
+++ b/solution.py
@@ -71,7 +71,10 @@
     flattened = pieces.reshape(-1, pieces.shape[-1])
     product = jnp.dot(flattened, out_proj, preferred_element_type=jnp.float32).astype(jnp.bfloat16)
     columns = product.reshape(pieces.shape[:-1] + (out_proj.shape[1],))
-    projected = lax.all_to_all(columns, "dp", split_axis=1, concat_axis=3, tiled=True)[0, 0]
+    projected = jnp.concatenate(
+        lax.all_to_all(jnp.stack(jnp.split(columns, lax.axis_size("dp"), axis=1)), "dp", 0, 0),
+        axis=3,
+    )[0, 0]
     stream_in = residual[0, 0].astype(jnp.float32) + projected.astype(jnp.float32)
     normal_rows = rms_scale(stream_in, gain_in).astype(jnp.bfloat16)
     column = gather_axis(normal_rows, "dp", 0)

time: 130 us -> 127 us (0.977)
  matrix products: 19.9 us -> 17.6 us
  waiting for transfers between devices: 35.2 us -> 37.4 us
  other arithmetic: 7.4 us -> 5.66 us
    ppermute x5, waiting for transfers between devices: 16.4 us -> 18.2 us  [gather_axis(): lax.ppermute(x, name, [(j, (j + shift) % n) for j in range(n)])]
    dot_general x4, matrix products: 9.61 us -> 7.97 us  [by_rows(): lax.dot_general(left, weight_rows, (((1,), (1,)), ((), ())), preferred_el...]
  transfers between devices with their start and end apart: 8 -> 8, of which waited for: 5 -> 6; matrix products, arithmetic and copies ran while one was open for 10% -> 11% of each run, Pallas kernels for 0% -> 0%
where the time goes in v1:
time: 127 us; the launch traced here: 126 us
  blocking collectives  41.9 us (33%)
  waiting for transfers between devices  37.4 us (29%)
  matrix products  17.6 us (14%)
  starting transfers between devices  16.8 us (13%)
  local copies, waits for them, and re-layouts  5.89 us (5%)
  other arithmetic  5.66 us (4%)
    all_to_all x1, blocking collectives, shards(): lax.all_to_all(outgoing, 'expert', split_axis=0, concat_axis=0, tiled=True)  41.9 us
    ppermute x5, waiting for transfers between devices, gather_axis(): lax.ppermute(x, name, [(j, (j + shift) % n) for j in range(n)])  18.2 us
    all_to_all x1, waiting for transfers between devices, shards(): lax.all_to_all(expert_out, 'expert', split_axis=0, concat_axis=0, tiled=T...  10.8 us
    dot_general x4, matrix products, by_rows(): lax.dot_general(left, weight_rows, (((1,), (1,)), ((), ())), preferred_el...  7.97 us
    ppermute x5, starting transfers between devices, gather_axis(): lax.ppermute(x, name, [(j, (j + shift) % n) for j in range(n)])  5.5 us
    all_to_all x1, starting transfers between devices, shards(): lax.all_to_all(expert_out, 'expert', split_axis=0, concat_axis=0, tiled=T...  4.6 us
    all_to_all x1, waiting for transfers between devices, shards(): lax.all_to_all(combined, 'dp', split_axis=0, concat_axis=2, tiled=True)[0]  4.3 us
    all_to_all x1, waiting for transfers between devices, shards(): lax.all_to_all(jnp.stack(jnp.split(columns, lax.axis_size('dp'), axis=1))...  4.09 us
  transfers between devices with their start and end apart: 8, of which 6 were waited for; matrix products, arithmetic and copies ran while one was open for 11% of the time, Pallas kernels for 0%

profile of v1, /device:TPU:0, one launch (start us, length us, event | category | flops | bytes accessed | tf_op | source)
XLA Modules:
  0.0 126.1 jit_solution(8882846075183960452)
XLA Ops:
  0.6 3.0 %collective-permute-start = (bf16[1,1,16,1024]{3,2,1,0:T(8,128)(2,1)}, bf16[1,1,16,1024]{3,2,1,0:T(8,128)(2,1)S(1)}, u32[]{:S(2)}, u32[]{:S(2)}) collective-permute-start(bf16[1,1,16,1024]{3,2,1,0:T(8,128)(2,1)} %param.14), channel_id=1, source_target_pairs={{0,16},{16,0},{1,17},{17,1},{2,18},{18,2},{3,19},{19,3},{4,20},{20... | collective-permute-start | bytes 98312 | tf_op jit(solution)/shard_map/ppermute | solution.py:28
  4.6 0.8 copy.45
  7.7 0.8 broadcast_select_fusion.7
  8.5 2.1 %convolution_convert_fusion.1 = bf16[32,1024]{1,0:T(8,128)(2,1)S(1)} fusion(bf16[32,1024]{1,0:T(8,128)(2,1)S(1)} %bitcast.87, bf16[1024,1024]{1,0:T(8,128)(2,1)} %param.16), kind=kOutput, calls=%fused_computation.13 | convolution fusion | flops 67141632 | bytes 2228224 | tf_op jit(solution)/shard_map/dot_general | solution.py:72
  11.3 3.3 %all-to-all-start = ((bf16[2,1,1,16,1024]{4,3,2,1,0:T(8,128)(2,1)}), bf16[2,1,1,16,1024]{4,3,2,1,0:T(8,128)(2,1)S(1)}, u32[]{:S(2)}, u32[]{:S(2)}) async-start(bf16[2,1,1,16,1024]{4,3,2,1,0:T(8,128)(2,1)} %pad_maximum_fusion.2), calls=%async_computation | async-start | bytes 131072 | tf_op jit(solution)/shard_map/all_to_all | solution.py:75
  14.6 4.1 %all-to-all-done = bf16[2,1,1,16,1024]{4,3,2,1,0:T(8,128)(2,1)S(1)} async-done(((bf16[2,1,1,16,1024]{4,3,2,1,0:T(8,128)(2,1)}), bf16[2,1,1,16,1024]{4,3,2,1,0:T(8,128)(2,1)S(1)}, u32[]{:S(2)}, u32[]{:S(2)}) %all-to-all-start) | async-done | bytes 65568 | tf_op jit(solution)/shard_map/all_to_all | solution.py:75
  19.3 4.1 %collective-permute-done.1 = bf16[16,2048]{1,0:T(8,128)(2,1)S(1)} collective-permute-done((bf16[16,2048]{1,0:T(8,128)(2,1)S(1)}, bf16[16,2048]{1,0:T(8,128)(2,1)S(1)}, u32[]{:S(2)}, u32[]{:S(2)}) %collective-permute-start.1) | collective-permute-done | bytes 65568 | tf_op jit(solution)/shard_map/ppermute | solution.py:28
  24.1 41.9 %all_to_all.30 = bf16[16,24,2048]{2,1,0:T(8,128)(2,1)S(1)} all-to-all(bf16[16,24,2048]{2,1,0:T(8,128)(2,1)S(1)} %bitcast.77), channel_id=1, replica_groups=mesh['dp'=2,'expert'=16] {'expert'}, dimensions={0} | all-to-all | bytes 3145728 | tf_op jit(solution)/shard_map/all_to_all | solution.py:110
  66.0 1.7 %fusion.4 = f32[384,704]{0,1:T(8,128)S(1)} fusion(bf16[384,2048]{1,0:T(8,128)(2,1)S(1)} %bitcast.78, bf16[1,704,2048]{2,1,0:T(8,128)(2,1)S(1)} %copy-done.8), kind=kOutput, calls=%fused_computation.5 | convolution fusion | flops 1107296256 | bytes 5537792 | tf_op jit(solution)/shard_map/dot_general | solution.py:16
  67.8 2.5 %fusion.12 = bf16[384,704]{0,1:T(8,128)(2,1)} fusion(bf16[384,2048]{1,0:T(8,128)(2,1)S(1)} %bitcast.79, bf16[1,704,2048]{2,1,0:T(8,128)(2,1)S(1)} %copy-done.9, f32[384,704]{0,1:T(8,128)S(1)} %fusion.4), kind=kOutput, calls=%fused_computation.10 | convolution fusion | flops 1108918272 | bytes 6078464 | tf_op jit(solution)/shard_map/dot_general | solution.py:16
  70.8 2.0 %collective-permute-start.2 = (f32[32,8]{0,1:T(8,128)S(1)}, f32[32,8]{0,1:T(8,128)S(1)}, u32[]{:S(2)}, u32[]{:S(2)}) collective-permute-start(f32[32,8]{0,1:T(8,128)S(1)} %fusion.41), channel_id=1, source_target_pairs={{0,16},{16,0},{1,17},{17,1},{2,18},{18,2},{3,19},{19,3},{4,20},{20... | collective-permute-start | bytes 3080 | tf_op jit(solution)/shard_map/ppermute | solution.py:28
  72.8 12.8 %collective-permute-done.3 = bf16[384,704]{0,1:T(8,128)(2,1)} collective-permute-done((bf16[384,704]{0,1:T(8,128)(2,1)}, bf16[384,704]{0,1:T(8,128)(2,1)}, u32[]{:S(2)}, u32[]{:S(2)}) %collective-permute-start.3) | collective-permute-done | bytes 540704 | tf_op jit(solution)/shard_map/ppermute | solution.py:28
  85.7 1.3 %broadcast_select_fusion.1 = (bf16[384,704]{0,1:T(8,128)(2,1)S(1)}, bf16[384,704]{0,1:T(8,128)(2,1)S(1)}) fusion(bf16[384,704]{0,1:T(8,128)(2,1)} %fusion.12, bf16[384,704]{0,1:T(8,128)(2,1)} %collective-permute-done.3, pred[]{:T(512)S(6)} %eq.16), kind=kLoop, calls=%fused_computation.18 | loop fusion | flops 540672 | bytes 2162689 | tf_op jit(solution)/shard_map/jit(_where)/select_n | solution.py:30
  87.0 2.3 %fusion.6 = bf16[384,1024]{1,0:T(8,128)(2,1)} fusion(bf16[1,1408,1024]{2,1,0:T(8,128)(2,1)S(1)} %copy-done, bf16[384,704]{0,1:T(8,128)(2,1)S(1)} %get-tuple-element.3, bf16[384,704]{0,1:T(8,128)(2,1)S(1)} %get-tuple-element.2), kind=kOutput, calls=%fused_computation.8 | convolution fusion | flops 1109852160 | bytes 4751360 | tf_op jit(solution)/shard_map/dot_general | solution.py:120
  89.3 4.6 %all-to-all-start.2 = ((bf16[16,24,1024]{2,1,0:T(8,128)(2,1)}), bf16[16,24,1024]{2,1,0:T(8,128)(2,1)}, u32[]{:S(2)}, u32[]{:S(2)}) async-start(bf16[16,24,1024]{2,1,0:T(8,128)(2,1)} %bitcast.83), calls=%async_computation.2 | async-start | bytes 1572864 | tf_op jit(solution)/shard_map/all_to_all | solution.py:123
  93.9 2.9 %fusion.40 = f32[32,704]{1,0:T(8,128)S(1)} fusion(bf16[704,2048]{1,0:T(8,128)(2,1)} %param.24, bf16[16,2048]{1,0:T(8,128)(2,1)S(1)} %get-tuple-element.7, bf16[16,2048]{1,0:T(8,128)(2,1)S(1)} %get-tuple-element.6), kind=kOutput, calls=%fused_computation.77 | convolution fusion | flops 92536832 | bytes 3104768 | tf_op jit(solution)/shard_map/dot_general | solution.py:16
  96.8 0.9 multiply_convert_fusion.2
  98.1 1.7 %gather_fusion = f32[192]{0:T(256)S(1)} fusion(f32[32,16]{0,1:T(8,128)S(1)} %pad_maximum_fusion.3, s32[192]{0:T(256)S(1)} %reshape.294), kind=kCustom, calls=%fused_computation | custom fusion | bytes 3072 | tf_op jit(solution)/shard_map/jit(take_along_axis)/gather | solution.py:84
  100.7 1.2 collective-permute-done.4
  101.9 10.8 %all-to-all-done.2 = bf16[16,24,1024]{2,1,0:T(8,128)(2,1)} async-done(((bf16[16,24,1024]{2,1,0:T(8,128)(2,1)}), bf16[16,24,1024]{2,1,0:T(8,128)(2,1)}, u32[]{:S(2)}, u32[]{:S(2)}) %all-to-all-start.2) | async-done | bytes 786464 | tf_op jit(solution)/shard_map/all_to_all | solution.py:123
  112.7 1.4 %fusion.42 = f32[32,1024]{1,0:T(8,128)S(1)} fusion(bf16[32,384]{1,0:T(8,128)(2,1)S(1)} %fusion.21, bf16[384,1024]{1,0:T(8,128)(2,1)} %bitcast.13), kind=kOutput, calls=%fused_computation.79 | convolution fusion | flops 25165824 | bytes 942080 | tf_op jit(solution)/shard_map/dot_general | solution.py:129
  114.0 3.1 %fusion.15 = f32[32,1024]{1,0:T(8,128)} fusion(f32[32,1024]{1,0:T(8,128)S(1)} %fusion.42, bf16[1408,1024]{1,0:T(8,128)(2,1)} %param.26, bf16[32,704]{1,0:T(8,128)(2,1)S(1)} %get-tuple-element.9, bf16[32,704]{1,0:T(8,128)(2,1)S(1)} %get-tuple-element.8, pred[32]{0:T(512)(128)(4,1)S(1)} %lt.57), kind=kOutput, calls=%fused_computation.12 | convolution fusion | flops 92520448 | bytes 3235872 | tf_op jit(solution)/shard_map/dot_general | solution.py:121
  117.2 3.4 %all-to-all-start.3 = ((f32[2,16,1024]{2,1,0:T(8,128)}), f32[2,16,1024]{2,1,0:T(8,128)S(1)}, u32[]{:S(2)}, u32[]{:S(2)}) async-start(f32[2,16,1024]{2,1,0:T(8,128)} %bitcast.14), calls=%async_computation.3 | async-start | bytes 262144 | tf_op jit(solution)/shard_map/all_to_all | solution.py:133
  120.7 4.3 %all-to-all-done.3 = f32[2,16,1024]{2,1,0:T(8,128)S(1)} async-done(((f32[2,16,1024]{2,1,0:T(8,128)}), f32[2,16,1024]{2,1,0:T(8,128)S(1)}, u32[]{:S(2)}, u32[]{:S(2)}) %all-to-all-start.3) | async-done | bytes 131104 | tf_op jit(solution)/shard_map/all_to_all | solution.py:133
  (79 shorter events, 8.2 us)
Async XLA Ops:
  0.6 86.4 %copy-start = (bf16[1,1408,1024]{2,1,0:T(8,128)(2,1)S(1)}, bf16[1,1408,1024]{2,1,0:T(8,128)(2,1)}, u32[]{:S(2)}) copy-start(bf16[1,1408,1024]{2,1,0:T(8,128)(2,1)} %param.23) | copy-start | bytes 8650756
  0.6 7.1 %collective-permute-start = (bf16[1,1,16,1024]{3,2,1,0:T(8,128)(2,1)}, bf16[1,1,16,1024]{3,2,1,0:T(8,128)(2,1)S(1)}, u32[]{:S(2)}, u32[]{:S(2)}) collective-permute-start(bf16[1,1,16,1024]{3,2,1,0:T(8,128)(2,1)} %param.14), channel_id=1, source_target_pairs={{0,16},{16,0},{1,17},{17,1},{2,18},{18,2},{3,19},{19,3},{4,20},{20... | collective-permute-start | bytes 98312 | tf_op jit(solution)/shard_map/ppermute | solution.py:28
  5.4 0.6 copy-start.3
  6.0 12.8 %copy-start.2 = (bf16[1,1,16,2048]{3,2,1,0:T(8,128)(2,1)S(1)}, bf16[1,1,16,2048]{3,2,1,0:T(8,128)(2,1)}, u32[]{:S(2)}) copy-start(bf16[1,1,16,2048]{3,2,1,0:T(8,128)(2,1)} %param.15) | copy-start | bytes 196612
  6.3 12.7 %copy-start.7 = (f32[2048]{0:T(1024)S(1)}, f32[2048]{0:T(1024)}, u32[]{:S(2)}) copy-start(f32[2048]{0:T(1024)} %param.17) | copy-start | bytes 24580
  11.3 7.4 %all-to-all-start = ((bf16[2,1,1,16,1024]{4,3,2,1,0:T(8,128)(2,1)}), bf16[2,1,1,16,1024]{4,3,2,1,0:T(8,128)(2,1)S(1)}, u32[]{:S(2)}, u32[]{:S(2)}) async-start(bf16[2,1,1,16,1024]{4,3,2,1,0:T(8,128)(2,1)} %pad_maximum_fusion.2), calls=%async_computation | async-start | bytes 131072 | tf_op jit(solution)/shard_map/all_to_all | solution.py:75
  19.1 4.3 %collective-permute-start.1 = (bf16[16,2048]{1,0:T(8,128)(2,1)S(1)}, bf16[16,2048]{1,0:T(8,128)(2,1)S(1)}, u32[]{:S(2)}, u32[]{:S(2)}) collective-permute-start(bf16[16,2048]{1,0:T(8,128)(2,1)S(1)} %multiply_convert_fusion.1), channel_id=1, source_target_pairs={{0,16},{16,0},{1,17},{17,1},{2,18},{18,2},{3,19},{19,3},{4,20},{20... | collective-permute-start | bytes 196616 | tf_op jit(solution)/shard_map/ppermute | solution.py:28
  23.5 42.6 %copy-start.8 = (bf16[1,704,2048]{2,1,0:T(8,128)(2,1)S(1)}, bf16[1,704,2048]{2,1,0:T(8,128)(2,1)}, u32[]{:S(2)}) copy-start(bf16[1,704,2048]{2,1,0:T(8,128)(2,1)} %param.21) | copy-start | bytes 8650756
  66.0 1.8 %copy-start.9 = (bf16[1,704,2048]{2,1,0:T(8,128)(2,1)S(1)}, bf16[1,704,2048]{2,1,0:T(8,128)(2,1)}, u32[]{:S(2)}) copy-start(bf16[1,704,2048]{2,1,0:T(8,128)(2,1)} %param.22) | copy-start | bytes 8650756
  67.8 2.5 %copy-start.5 = (s32[1,2,16,6]{2,1,3,0:T(2,128)S(1)}, s32[1,2,16,6]{2,1,3,0:T(2,128)}, u32[]{:S(2)}) copy-start(s32[1,2,16,6]{2,1,3,0:T(2,128)} %param.19) | copy-start | bytes 2308
  67.8 2.8 %copy-start.10 = (bf16[2048,8]{0,1:T(8,128)(2,1)S(1)}, bf16[2048,8]{0,1:T(8,128)(2,1)}, u32[]{:S(2)}) copy-start(bf16[2048,8]{0,1:T(8,128)(2,1)} %param.18) | copy-start | bytes 98308
  70.3 15.3 %collective-permute-start.3 = (bf16[384,704]{0,1:T(8,128)(2,1)}, bf16[384,704]{0,1:T(8,128)(2,1)}, u32[]{:S(2)}, u32[]{:S(2)}) collective-permute-start(bf16[384,704]{0,1:T(8,128)(2,1)} %fusion.12), channel_id=1, source_target_pairs={{0,16},{16,0},{1,17},{17,1},{2,18},{18,2},{3,19},{19,3},{4,20},{20... | collective-permute-start | bytes 1622024 | tf_op jit(solution)/shard_map/ppermute | solution.py:28
  70.8 27.3 %collective-permute-start.2 = (f32[32,8]{0,1:T(8,128)S(1)}, f32[32,8]{0,1:T(8,128)S(1)}, u32[]{:S(2)}, u32[]{:S(2)}) collective-permute-start(f32[32,8]{0,1:T(8,128)S(1)} %fusion.41), channel_id=1, source_target_pairs={{0,16},{16,0},{1,17},{17,1},{2,18},{18,2},{3,19},{19,3},{4,20},{20... | collective-permute-start | bytes 3080 | tf_op jit(solution)/shard_map/ppermute | solution.py:28
  89.3 23.4 %all-to-all-start.2 = ((bf16[16,24,1024]{2,1,0:T(8,128)(2,1)}), bf16[16,24,1024]{2,1,0:T(8,128)(2,1)}, u32[]{:S(2)}, u32[]{:S(2)}) async-start(bf16[16,24,1024]{2,1,0:T(8,128)(2,1)} %bitcast.83), calls=%async_computation.2 | async-start | bytes 1572864 | tf_op jit(solution)/shard_map/all_to_all | solution.py:123
  93.9 2.9 %copy-start.1 = (bf16[704,2048]{1,0:T(8,128)(2,1)S(1)}, bf16[704,2048]{1,0:T(8,128)(2,1)}, u32[]{:S(2)}) copy-start(bf16[704,2048]{1,0:T(8,128)(2,1)} %param.25) | copy-start | bytes 8650756
  97.7 4.2 %collective-permute-start.4 = (bf16[32,704]{1,0:T(8,128)(2,1)S(1)}, bf16[32,704]{1,0:T(8,128)(2,1)S(1)}, u32[]{:S(2)}, u32[]{:S(2)}) collective-permute-start(bf16[32,704]{1,0:T(8,128)(2,1)S(1)} %multiply_convert_fusion.2), channel_id=1, source_target_pairs={{0,16},{16,0},{1,17},{17,1},{2,18},{18,2},{3,19},{19,3},{4,20},{20... | collective-permute-start | bytes 135176 | tf_op jit(solution)/shard_map/ppermute | solution.py:28
  98.1 1.9 %copy-start.4 = (s32[1,2,16,6]{3,2,1,0:T(8,128)S(1)}, s32[1,2,16,6]{3,2,1,0:T(8,128)}, u32[]{:S(2)}) copy-start(s32[1,2,16,6]{3,2,1,0:T(8,128)} %copy-done.3) | copy-start | bytes 2308
  114.0 11.4 %copy-start.6 = (f32[2048]{0:T(1024)S(1)}, f32[2048]{0:T(1024)}, u32[]{:S(2)}) copy-start(f32[2048]{0:T(1024)} %param.27) | copy-start | bytes 24580
  117.2 7.8 %all-to-all-start.3 = ((f32[2,16,1024]{2,1,0:T(8,128)}), f32[2,16,1024]{2,1,0:T(8,128)S(1)}, u32[]{:S(2)}, u32[]{:S(2)}) async-start(f32[2,16,1024]{2,1,0:T(8,128)} %bitcast.14), calls=%async_computation.3 | async-start | bytes 262144 | tf_op jit(solution)/shard_map/all_to_all | solution.py:133
